TPU v7x, 128 devices: a whole 4x4x4 slice. The times are simulated.
128 devices in a mesh: row: 8 (over y, core), col: 16 (over z, x).
Axes of the slice: x: 4, y: 4, z: 4, core: 2. Of those that a mesh axis runs over, the one named last changes fastest.
Arguments:
- fock: bfloat16 [32768, 16, 2048], P('row', 'col'), may hold values from -6 to 6
- lmo_coef: bfloat16 [32768, 1024], P(('row', 'col')), may hold values from -0.078125 to 0.078125
- three_index: bfloat16 [32768, 512], P(('row', 'col')), may hold values from -6 to 6
- rotation: bfloat16 [16, 8, 1024, 512], P('col', 'row'), may hold values from -0.1875 to 0.1875
- lmo_ids: int32 [16, 8], replicated, may hold values from 0 to 127, as said below
- domains: int32 [128, 8], replicated, may hold values from -1 to 255, as said below
Outputs:
- proj_fock: float32 [16, 8, 512, 512], P('col', 'row')
- three_rot: bfloat16 [16, 8, 512, 512], P('col', 'row')
Inputs may be any that keep to these rules, and one draw needn't show every extreme that they name: `lmo_ids`: every LMO number appears exactly once; row o lists the 8 LMOs owned by column set o. `domains`: entry k of a list is -1 or a block of row panel k; entry 0 is never -1. The present blocks of one list lie in distinct column sets. For one owner o and one entry k, the blocks of the lists of lmo_ids[o, j] over all j lie in distinct column sets; for one j and one entry k, those of lmo_ids[o, j] over all o do too.
All inputs are finite; a program needn't handle non-finite values.
Results may differ from a plain program's by a relative error of at most 0.02.
Values may be sent and summed in bfloat16 or wider, within the bound.
No kernel may reach another device: no remote copies, remote signals or barrier semaphores. Data moves between devices by JAX's collectives and lax.ppermute only.
A program may use at most 192 MiB of HBM per device.

v0:
```python
import jax
import jax.numpy as jnp
from jax import lax
from jax.sharding import PartitionSpec as P

BLK = 128
F32 = jnp.float32
BF16 = jnp.bfloat16


def pick(mask, table):
    return jnp.sum(jnp.where(mask, table, 0), axis=-1)


def body(fock, lmo_coef, three_index, rotation, lmo_ids, domains):
    num_sets = lax.axis_size("col")
    my_row = lax.axis_index("row")
    my_col = lax.axis_index("col")
    dev_rows = lmo_coef.shape[0]
    occ_width = lmo_coef.shape[1]
    dev_blocks = dev_rows // BLK
    dom_blocks = domains.shape[1]
    dom_width = dom_blocks * BLK
    panel_fock = fock[:, 0, :]
    panel_blocks = panel_fock.shape[0] // BLK
    col_blocks = panel_fock.shape[1] // BLK
    doms = jnp.take(domains, lmo_ids, axis=0)
    present = doms >= 0
    clipped = jnp.maximum(doms, 0)
    flat = clipped // dev_blocks
    cset = flat % num_sets
    sub = clipped % dev_blocks
    panel = flat // num_sets
    row_tile = cset * dev_blocks + sub
    col_tile = panel * dev_blocks + sub
    pres_k = lax.dynamic_index_in_dim(present, my_row, 2, keepdims=False)
    cset_k = lax.dynamic_index_in_dim(cset, my_row, 2, keepdims=False)
    sub_k = lax.dynamic_index_in_dim(sub, my_row, 2, keepdims=False)
    rtile_k = lax.dynamic_index_in_dim(row_tile, my_row, 2, keepdims=False)
    mine_k = pres_k & (cset_k == my_col)
    sub_o = pick(mine_k, sub_k)
    mine2 = present & (cset == my_col)
    ct = pick(mine2, col_tile)
    fock_tiles = panel_fock.reshape(panel_blocks, BLK, col_blocks, BLK)
    tiles_a = fock_tiles.at[rtile_k, :, ct, :].get(mode="promise_in_bounds")
    in_rows = jnp.concatenate([lmo_coef, three_index], axis=1).reshape(dev_blocks, BLK, -1)
    rows_a = jnp.take(in_rows, sub_o, axis=0, mode="clip")
    rows_a = lax.all_to_all(rows_a, "col", 0, 0, tiled=True)
    tiles_a, rows_a = lax.optimization_barrier((tiles_a, rows_a))
    tiles_a = lax.all_to_all(tiles_a, "col", 0, 0, tiled=True)
    gathered = lax.all_gather(lmo_coef, "row", axis=0, tiled=True)
    fock_lmo = jnp.dot(panel_fock, gathered, preferred_element_type=F32).astype(BF16)
    rows_a, tiles_a, fock_lmo = lax.optimization_barrier((rows_a, tiles_a, fock_lmo))
    coef_b = lax.psum_scatter(fock_lmo, "col", scatter_dimension=0, tiled=True)
    occ_term = jnp.einsum("ri,rj->ij", lmo_coef, coef_b, preferred_element_type=F32)
    occ_b = lax.psum(occ_term, ("row", "col")).astype(BF16)
    pres_o = lax.dynamic_index_in_dim(present, my_col, 0, keepdims=False)
    cset_o = lax.dynamic_index_in_dim(cset, my_col, 0, keepdims=False)
    pres_jk = lax.dynamic_index_in_dim(pres_o, my_row, 1, keepdims=False)
    cset_jk = lax.dynamic_index_in_dim(cset_o, my_row, 1, keepdims=False)
    rows_b = jnp.take(rows_a, cset_jk, axis=0, mode="clip")
    rows_b = jnp.where(pres_jk[:, None, None], rows_b, jnp.zeros_like(rows_b))
    slot_ids = jnp.broadcast_to(jnp.arange(dom_blocks, dtype=jnp.int32)[:, None], cset_o.shape)
    tiles_b = tiles_a.at[cset_o, slot_ids].get(mode="promise_in_bounds")
    live_b = pres_o & pres_jk[:, None]
    tiles_b = jnp.where(live_b[:, :, None, None], tiles_b, jnp.zeros_like(tiles_b))
    rows_dom, tiles_dom = (
        lax.all_to_all(rows_b, "row", 0, 0, tiled=True),
        lax.all_to_all(tiles_b, "row", 0, 0, tiled=True),
    )
    rows_dom = rows_dom.reshape(dom_width, -1)
    fc_a = jnp.take(coef_b.reshape(dev_blocks, BLK, occ_width), sub_o, axis=0, mode="clip")
    fc_a = lax.all_to_all(fc_a, "col", 0, 0, tiled=True)
    fc_a, occ_b, rows_dom, tiles_dom = lax.optimization_barrier((fc_a, occ_b, rows_dom, tiles_dom))
    fc_b = jnp.take(fc_a, cset_jk, axis=0, mode="clip")
    fc_b = jnp.where(pres_jk[:, None, None], fc_b, jnp.zeros_like(fc_b))
    fc_dom = lax.all_to_all(fc_b, "row", 0, 0, tiled=True).reshape(dom_width, occ_width)
    coef_dom = rows_dom[:, :occ_width]
    three_dom = rows_dom[:, occ_width:]
    correction = jnp.dot(coef_dom, occ_b, preferred_element_type=F32)
    proj_dom = (fc_dom.astype(F32) - 0.5 * correction).astype(BF16)
    slot_rot = rotation[0, 0]
    rot_tiles = slot_rot.reshape(dom_blocks, BLK, -1)
    fock_half = jnp.einsum("abtu,bun->atn", tiles_dom, rot_tiles, preferred_element_type=F32)
    fock_half = fock_half.reshape(dom_width, -1).astype(BF16)
    fock_rot = jnp.einsum("xm,xn->mn", slot_rot, fock_half, preferred_element_type=F32)
    coef_rot = jnp.einsum("xm,xi->mi", slot_rot, coef_dom, preferred_element_type=F32).astype(BF16)
    proj_rot = jnp.einsum("xm,xi->mi", slot_rot, proj_dom, preferred_element_type=F32).astype(BF16)
    proj_fock = fock_rot - jnp.einsum("mi,ni->mn", coef_rot, proj_rot, preferred_element_type=F32)
    proj_fock = proj_fock - jnp.einsum("mi,ni->mn", proj_rot, coef_rot, preferred_element_type=F32)
    three_rot = jnp.einsum("xm,xu->mu", slot_rot, three_dom, preferred_element_type=F32).astype(
        BF16
    )
    return (proj_fock[None, None], three_rot[None, None])


def solution(mesh):
    placed = (
        P("row", "col", None),
        P(("row", "col"), None),
        P(("row", "col"), None),
        P("col", "row", None, None),
        P(),
        P(),
    )
    return jax.shard_map(
        body,
        mesh=mesh,
        in_specs=placed,
        out_specs=(P("col", "row", None, None), P("col", "row", None, None)),
        check_vma=False,
    )
```

profile of v0, /device:TPU:1, one launch (start us, length us, event | category | flops | bytes accessed | tf_op | source)
XLA Modules:
  0.0 483.2 jit_solution(15179841917422128813)
XLA Ops:
  12.3 3.6 gather_fusion.2
  15.9 8.5 %all-to-all-start = ((bf16[16,128,1536]{2,1,0:T(8,128)(2,1)}), bf16[16,128,1536]{2,1,0:T(8,128)(2,1)}, u32[]{:S(2)}, u32[]{:S(2)}) async-start(bf16[16,128,1536]{2,1,0:T(8,128)(2,1)} %gather_fusion.2), calls=%async_computation | async-start | bytes 12582912 | tf_op jit(solution)/shard_map/all_to_all | solution.py:48
  24.4 9.7 %copy.44 = bf16[512,8,16,128]{3,2,1,0:T(8,128)(2,1)S(1)} copy(bf16[512,8,16,128]{3,1,2,0:T(8,128)(2,1)} %bitcast.68) | data formatting | bytes 33554432
  34.1 8.2 %copy.33 = bf16[32,128,16,128]{3,1,2,0:T(8,128)(2,1)} copy(bf16[32,128,16,128]{3,2,1,0:T(8,128)(2,1)S(1)} %bitcast.65) | data formatting | bytes 33554432 | tf_op jit(solution)/shard_map/reshape;squeeze | solution.py:44
  42.5 9.0 %gather_fusion.1 = bf16[128,128,128]{2,1,0:T(8,128)(2,1)} fusion(bf16[32,128,16,128]{3,1,2,0:T(8,128)(2,1)} %copy.33, s32[128]{0:T(128)S(1)} %reshape.121), kind=kCustom, calls=%fused_computation.1 | custom fusion | bytes 8389632 | tf_op jit(solution)/shard_map/gather | solution.py:45
  51.5 65.2 %all-to-all-done = bf16[16,128,1536]{2,1,0:T(8,128)(2,1)} async-done(((bf16[16,128,1536]{2,1,0:T(8,128)(2,1)}), bf16[16,128,1536]{2,1,0:T(8,128)(2,1)}, u32[]{:S(2)}, u32[]{:S(2)}) %all-to-all-start) | async-done | bytes 6291488 | tf_op jit(solution)/shard_map/all_to_all | solution.py:48
  116.7 5.4 %all-to-all-start.1 = ((bf16[16,8,128,128]{3,2,1,0:T(8,128)(2,1)}), bf16[16,8,128,128]{3,2,1,0:T(8,128)(2,1)}, u32[]{:S(2)}, u32[]{:S(2)}) async-start(bf16[16,8,128,128]{3,2,1,0:T(8,128)(2,1)} %bitcast.69), calls=%async_computation.1 | async-start | bytes 8388608 | tf_op jit(solution)/shard_map/all_to_all | solution.py:50
  122.2 23.4 %fusion.2 = bf16[4096,1024]{1,0:T(8,128)(2,1)} fusion(bf16[2048,1024]{1,0:T(8,128)(2,1)} %all-gather.2.cloned.1.call-done, bf16[4096,1,2048]{2,0,1:T(8,128)(2,1)} %param.6), kind=kOutput, calls=%fused_computation.9 | convolution fusion | flops 17184063488 | bytes 29360128 | tf_op jit(solution)/shard_map/dot_general | solution.py:52
  145.7 35.7 %all-to-all-done.1 = bf16[16,8,128,128]{3,2,1,0:T(8,128)(2,1)} async-done(((bf16[16,8,128,128]{3,2,1,0:T(8,128)(2,1)}), bf16[16,8,128,128]{3,2,1,0:T(8,128)(2,1)}, u32[]{:S(2)}, u32[]{:S(2)}) %all-to-all-start.1) | async-done | bytes 4194336 | tf_op jit(solution)/shard_map/all_to_all | solution.py:50
  182.2 3.2 gather_fusion.5
  188.2 7.4 %all-to-all-start.4 = ((bf16[8,8,128,128]{3,1,2,0:T(8,128)(2,1)}), bf16[8,8,128,128]{3,1,2,0:T(8,128)(2,1)S(1)}, u32[]{:S(2)}, u32[]{:S(2)}) async-start(bf16[8,8,128,128]{3,1,2,0:T(8,128)(2,1)} %copy_select_fusion), calls=%async_computation.5 | async-start | bytes 4194304 | tf_op jit(solution)/shard_map/all_to_all | solution.py:69
  195.8 5.4 %gather_fusion.4 = bf16[8,128,1536]{2,1,0:T(8,128)(2,1)} fusion(bf16[16,128,1536]{2,1,0:T(8,128)(2,1)} %all-to-all-done, s32[1024]{0:T(1024)S(1)} %pad_clamp_fusion), kind=kCustom, calls=%fused_computation.4 | custom fusion | bytes 6291488 | tf_op jit(solution)/shard_map/jit(_take)/gather | solution.py:61
  201.2 4.0 broadcast_select_fusion
  205.1 16.8 %all-to-all-done.4 = bf16[8,8,128,128]{3,1,2,0:T(8,128)(2,1)S(1)} async-done(((bf16[8,8,128,128]{3,1,2,0:T(8,128)(2,1)}), bf16[8,8,128,128]{3,1,2,0:T(8,128)(2,1)S(1)}, u32[]{:S(2)}, u32[]{:S(2)}) %all-to-all-start.4) | async-done | bytes 2097184 | tf_op jit(solution)/shard_map/all_to_all | solution.py:69
  223.2 5.2 %all-to-all-start.3 = ((bf16[8,128,1536]{2,1,0:T(8,128)(2,1)}), bf16[8,128,1536]{2,1,0:T(8,128)(2,1)}, u32[]{:S(2)}, u32[]{:S(2)}) async-start(bf16[8,128,1536]{2,1,0:T(8,128)(2,1)} %broadcast_select_fusion), calls=%async_computation.4 | async-start | bytes 6291456 | tf_op jit(solution)/shard_map/all_to_all | solution.py:68
  228.4 37.5 %reduce-scatter.2.cloned.1.call-done = bf16[256,1024]{1,0:T(8,128)(2,1)} async-done(((bf16[4096,1024]{1,0:T(8,128)(2,1)}), bf16[256,1024]{1,0:T(8,128)(2,1)}) %reduce-scatter.2.cloned.1.call-update) | async-done | bytes 524304 | tf_op jit(solution)/shard_map/reduce_scatter | solution.py:54
  266.0 3.8 gather_fusion.3
  269.8 4.9 %all-to-all-start.2 = ((bf16[16,128,1024]{2,1,0:T(8,128)(2,1)}), bf16[16,128,1024]{2,1,0:T(8,128)(2,1)}, u32[]{:S(2)}, u32[]{:S(2)}) async-start(bf16[16,128,1024]{2,1,0:T(8,128)(2,1)} %gather_fusion.3), calls=%async_computation.3 | async-start | bytes 8388608 | tf_op jit(solution)/shard_map/all_to_all | solution.py:73
  277.4 148.5 %all-reduce.1 = bf16[1024,1024]{0,1:T(8,128)(2,1)} all-reduce(f32[1024,1024]{0,1:T(8,128)} %convolution_bitcast_fusion), channel_id=1, replica_groups=mesh['row'=8,'col'=16] {'row','col'}, use_global_device_ids=true, to_apply=%region_3.4 | all-reduce | flops 1048576 | bytes 6291456 | tf_op jit(solution)/shard_map/psum | solution.py:56
  425.9 2.9 gather_fusion.6
  430.3 7.0 %all-to-all-start.5 = ((bf16[8,128,1024]{2,1,0:T(8,128)(2,1)}), bf16[8,128,1024]{2,1,0:T(8,128)(2,1)}, u32[]{:S(2)}, u32[]{:S(2)}) async-start(bf16[8,128,1024]{2,1,0:T(8,128)(2,1)} %broadcast_select_fusion.1), calls=%async_computation.6 | async-start | bytes 4194304 | tf_op jit(solution)/shard_map/all_to_all | solution.py:77
  443.2 4.3 convolution_bitcast_fusion.1
  447.6 16.3 %all-to-all-done.5 = bf16[8,128,1024]{2,1,0:T(8,128)(2,1)} async-done(((bf16[8,128,1024]{2,1,0:T(8,128)(2,1)}), bf16[8,128,1024]{2,1,0:T(8,128)(2,1)}, u32[]{:S(2)}, u32[]{:S(2)}) %all-to-all-start.5) | async-done | bytes 2097184 | tf_op jit(solution)/shard_map/all_to_all | solution.py:77
  463.8 6.3 %convolution_convert_fusion = bf16[1024,512]{1,0:T(8,128)(2,1)S(1)} fusion(bf16[1,1,1024,512]{3,2,1,0:T(8,128)(2,1)S(1)} %copy-done, bf16[1024,1024]{1,0:T(8,128)(2,1)} %bitcast.22, bf16[1024,1024]{0,1:T(8,128)(2,1)} %all-reduce.1, bf16[1024,1536]{1,0:T(8,128)(2,1)} %bitcast.7), kind=kOutput, calls=%fused_computation.23 | convolution fusion | flops 3225944064 | bytes 8388608 | tf_op jit(solution)/shard_map/xm,xi->mi/dot_general | solution.py:88
  (51 shorter events, 26.7 us)
Async XLA Ops:
  7.2 430.2 %copy-start = (bf16[1,1,1024,512]{3,2,1,0:T(8,128)(2,1)S(1)}, bf16[1,1,1024,512]{3,2,1,0:T(8,128)(2,1)}, u32[]{:S(2)}) copy-start(bf16[1,1,1024,512]{3,2,1,0:T(8,128)(2,1)} %param.9) | copy-start | bytes 3145732
  7.2 115.0 %all-gather.2.cloned.1.call-start = ((), (), s32[]{:S(2)}) async-start(), calls=%async_computation.7 | async-start | bytes 4718592 | tf_op jit(solution)/shard_map/all_gather | solution.py:51
  15.9 100.8 %all-to-all-start = ((bf16[16,128,1536]{2,1,0:T(8,128)(2,1)}), bf16[16,128,1536]{2,1,0:T(8,128)(2,1)}, u32[]{:S(2)}, u32[]{:S(2)}) async-start(bf16[16,128,1536]{2,1,0:T(8,128)(2,1)} %gather_fusion.2), calls=%async_computation | async-start | bytes 12582912 | tf_op jit(solution)/shard_map/all_to_all | solution.py:48
  116.7 64.7 %all-to-all-start.1 = ((bf16[16,8,128,128]{3,2,1,0:T(8,128)(2,1)}), bf16[16,8,128,128]{3,2,1,0:T(8,128)(2,1)}, u32[]{:S(2)}, u32[]{:S(2)}) async-start(bf16[16,8,128,128]{3,2,1,0:T(8,128)(2,1)} %bitcast.69), calls=%async_computation.1 | async-start | bytes 8388608 | tf_op jit(solution)/shard_map/all_to_all | solution.py:50
  122.1 143.8 %reduce-scatter.2.cloned.1.call-start = ((), (), s32[]{:S(2)}) async-start(), calls=%async_computation.8 | async-start | bytes 8912896 | tf_op jit(solution)/shard_map/reduce_scatter | solution.py:54
  188.2 33.8 %all-to-all-start.4 = ((bf16[8,8,128,128]{3,1,2,0:T(8,128)(2,1)}), bf16[8,8,128,128]{3,1,2,0:T(8,128)(2,1)S(1)}, u32[]{:S(2)}, u32[]{:S(2)}) async-start(bf16[8,8,128,128]{3,1,2,0:T(8,128)(2,1)} %copy_select_fusion), calls=%async_computation.5 | async-start | bytes 4194304 | tf_op jit(solution)/shard_map/all_to_all | solution.py:69
  221.9 1.3 copy-start.4
  223.2 46.6 %all-to-all-start.3 = ((bf16[8,128,1536]{2,1,0:T(8,128)(2,1)}), bf16[8,128,1536]{2,1,0:T(8,128)(2,1)}, u32[]{:S(2)}, u32[]{:S(2)}) async-start(bf16[8,128,1536]{2,1,0:T(8,128)(2,1)} %broadcast_select_fusion), calls=%async_computation.4 | async-start | bytes 6291456 | tf_op jit(solution)/shard_map/all_to_all | solution.py:68
  269.8 4.9 %copy-start.1 = (bf16[256,1024]{1,0:T(8,128)(2,1)S(1)}, bf16[256,1024]{1,0:T(8,128)(2,1)}, u32[]{:S(2)}) copy-start(bf16[256,1024]{1,0:T(8,128)(2,1)} %reduce-scatter.2.cloned.1.call-done) | copy-start | bytes 1572868
  269.8 4.9 %copy-start.2 = (bf16[256,1024]{1,0:T(8,128)(2,1)S(1)}, bf16[256,1024]{1,0:T(8,128)(2,1)}, u32[]{:S(2)}) copy-start(bf16[256,1024]{1,0:T(8,128)(2,1)} %param.7) | copy-start | bytes 1572868
  269.8 156.2 %all-to-all-start.2 = ((bf16[16,128,1024]{2,1,0:T(8,128)(2,1)}), bf16[16,128,1024]{2,1,0:T(8,128)(2,1)}, u32[]{:S(2)}, u32[]{:S(2)}) async-start(bf16[16,128,1024]{2,1,0:T(8,128)(2,1)} %gather_fusion.3), calls=%async_computation.3 | async-start | bytes 8388608 | tf_op jit(solution)/shard_map/all_to_all | solution.py:73
  430.3 33.5 %all-to-all-start.5 = ((bf16[8,128,1024]{2,1,0:T(8,128)(2,1)}), bf16[8,128,1024]{2,1,0:T(8,128)(2,1)}, u32[]{:S(2)}, u32[]{:S(2)}) async-start(bf16[8,128,1024]{2,1,0:T(8,128)(2,1)} %broadcast_select_fusion.1), calls=%async_computation.6 | async-start | bytes 4194304 | tf_op jit(solution)/shard_map/all_to_all | solution.py:77
  470.1 1.0 copy-start.3
Sparse Core Ops, SparseCore 0:
  9.7 35.7 all-gather.1
  181.5 84.3 reduce-scatter.1
where the time goes:
time: 484 us; the launch traced here: 483 us
  waiting for transfers between devices  172 us (36%)
  blocking collectives  149 us (31%)
  local copies, waits for them, and re-layouts  53 us (11%)
  matrix products  45.6 us (9%)
  starting transfers between devices  38.6 us (8%)
  between operations  14.2 us (3%)
  other arithmetic  11 us (2%)
    psum x1, blocking collectives, body(): occ_b = lax.psum(occ_term, ('row', 'col')).astype(BF16)  149 us
    all_to_all x1, waiting for transfers between devices, body(): rows_a = lax.all_to_all(rows_a, 'col', 0, 0, tiled=True)  65.2 us
    reduce_scatter x1, waiting for transfers between devices, body(): coef_b = lax.psum_scatter(fock_lmo, 'col', scatter_dimension=0, tiled=True)  37.5 us
    all_to_all x1, waiting for transfers between devices, body(): tiles_a = lax.all_to_all(tiles_a, 'col', 0, 0, tiled=True)  35.7 us
    dot_general x1, matrix products, body(): jnp.dot(panel_fock, gathered, preferred_element_type=F32).astype(BF16)  23.4 us
    all_to_all x1, waiting for transfers between devices, body(): lax.all_to_all(tiles_b, 'row', 0, 0, tiled=True)  16.8 us
    all_to_all x1, waiting for transfers between devices, body(): lax.all_to_all(fc_b, 'row', 0, 0, tiled=True).reshape(dom_width, occ_width)  16.3 us
    unnamed x14, local copies, waits for them, and re-layouts  15.1 us
  transfers between devices with their start and end apart: 8, of which 5 were waited for; matrix products, arithmetic and copies ran while one was open for 19% of the time, Pallas kernels for 0%

commit v1 on v0

--- a/solution.py
+++ b/solution.py
@@ -6,6 +6,12 @@
 BLK = 128
 F32 = jnp.float32
 BF16 = jnp.bfloat16
+
+
+def block_solve(chunk, lane_axis, bus_axis):
+    for dev in (lane_axis, bus_axis):
+        chunk = lax.psum(chunk, axis_name=dev)
+    return chunk
 
 
 def pick(mask, table):
@@ -53,7 +59,7 @@
     rows_a, tiles_a, fock_lmo = lax.optimization_barrier((rows_a, tiles_a, fock_lmo))
     coef_b = lax.psum_scatter(fock_lmo, "col", scatter_dimension=0, tiled=True)
     occ_term = jnp.einsum("ri,rj->ij", lmo_coef, coef_b, preferred_element_type=F32)
-    occ_b = lax.psum(occ_term, ("row", "col")).astype(BF16)
+    occ_b = block_solve(occ_term, lane_axis="col", bus_axis="row").astype(BF16)
     pres_o = lax.dynamic_index_in_dim(present, my_col, 0, keepdims=False)
     cset_o = lax.dynamic_index_in_dim(cset, my_col, 0, keepdims=False)
     pres_jk = lax.dynamic_index_in_dim(pres_o, my_row, 1, keepdims=False)

time: 484 us -> 499 us (1.031)
  waiting for transfers between devices: 172 us -> 278 us
  blocking collectives: 149 us -> 58.8 us
    psum x1, blocking collectives: 149 us -> 58.8 us  [block_solve(): chunk = lax.psum(chunk, axis_name=dev)]
    psum x0 -> x1, waiting for transfers between devices: none -> 85.6 us  [block_solve(): chunk = lax.psum(chunk, axis_name=dev)]
    reduce_scatter x1, waiting for transfers between devices: 37.5 us -> 70.6 us  [body(): coef_b = lax.psum_scatter(fock_lmo, 'col', scatter_dimension=0, tiled=True)]
    all_to_all x1, waiting for transfers between devices: 16.8 us -> 0.01 us  [body(): lax.all_to_all(tiles_b, 'row', 0, 0, tiled=True)]
    unnamed x14 -> x12, local copies, waits for them, and re-layouts: 15.1 us -> 13.8 us
  transfers between devices with their start and end apart: 8 -> 9, of which waited for: 5 -> 6; matrix products, arithmetic and copies ran while one was open for 19% -> 18% of each run, Pallas kernels for 0% -> 0%
where the time goes in v1:
time: 499 us; the launch traced here: 498 us
  waiting for transfers between devices  278 us (56%)
  blocking collectives  58.8 us (12%)
  local copies, waits for them, and re-layouts  50.6 us (10%)
  matrix products  46.6 us (9%)
  starting transfers between devices  39.2 us (8%)
  between operations  13.9 us (3%)
  other arithmetic  10.9 us (2%)
    psum x1, waiting for transfers between devices, block_solve(): chunk = lax.psum(chunk, axis_name=dev)  85.6 us
    reduce_scatter x1, waiting for transfers between devices, body(): coef_b = lax.psum_scatter(fock_lmo, 'col', scatter_dimension=0, tiled=True)  70.6 us
    all_to_all x1, waiting for transfers between devices, body(): rows_a = lax.all_to_all(rows_a, 'col', 0, 0, tiled=True)  65.2 us
    psum x1, blocking collectives, block_solve(): chunk = lax.psum(chunk, axis_name=dev)  58.8 us
    all_to_all x1, waiting for transfers between devices, body(): tiles_a = lax.all_to_all(tiles_a, 'col', 0, 0, tiled=True)  35.8 us
    dot_general x1, matrix products, body(): jnp.dot(panel_fock, gathered, preferred_element_type=F32).astype(BF16)  23.4 us
    all_to_all x1, waiting for transfers between devices, body(): lax.all_to_all(fc_b, 'row', 0, 0, tiled=True).reshape(dom_width, occ_width)  16.2 us
    unnamed x12, local copies, waits for them, and re-layouts  13.8 us
  transfers between devices with their start and end apart: 9, of which 6 were waited for; matrix products, arithmetic and copies ran while one was open for 18% of the time, Pallas kernels for 0%

profile of v1, /device:TPU:1, one launch (start us, length us, event | category | flops | bytes accessed | tf_op | source)
XLA Modules:
  0.0 497.7 jit_solution(10488451801915459138)
XLA Ops:
  12.3 3.6 gather_fusion.2
  15.9 8.5 %all-to-all-start = ((bf16[16,128,1536]{2,1,0:T(8,128)(2,1)}), bf16[16,128,1536]{2,1,0:T(8,128)(2,1)}, u32[]{:S(2)}, u32[]{:S(2)}) async-start(bf16[16,128,1536]{2,1,0:T(8,128)(2,1)} %gather_fusion.2), calls=%async_computation | async-start | bytes 12582912 | tf_op jit(solution)/shard_map/all_to_all | solution.py:54
  24.4 9.7 %copy.44 = bf16[512,8,16,128]{3,2,1,0:T(8,128)(2,1)S(1)} copy(bf16[512,8,16,128]{3,1,2,0:T(8,128)(2,1)} %bitcast.68) | data formatting | bytes 33554432
  34.1 8.2 %copy.33 = bf16[32,128,16,128]{3,1,2,0:T(8,128)(2,1)} copy(bf16[32,128,16,128]{3,2,1,0:T(8,128)(2,1)S(1)} %bitcast.65) | data formatting | bytes 33554432 | tf_op jit(solution)/shard_map/reshape;squeeze | solution.py:50
  42.5 9.0 %gather_fusion.1 = bf16[128,128,128]{2,1,0:T(8,128)(2,1)} fusion(bf16[32,128,16,128]{3,1,2,0:T(8,128)(2,1)} %copy.33, s32[128]{0:T(128)S(1)} %reshape.121), kind=kCustom, calls=%fused_computation.1 | custom fusion | bytes 8389632 | tf_op jit(solution)/shard_map/gather | solution.py:51
  51.5 65.2 %all-to-all-done = bf16[16,128,1536]{2,1,0:T(8,128)(2,1)} async-done(((bf16[16,128,1536]{2,1,0:T(8,128)(2,1)}), bf16[16,128,1536]{2,1,0:T(8,128)(2,1)}, u32[]{:S(2)}, u32[]{:S(2)}) %all-to-all-start) | async-done | bytes 6291488 | tf_op jit(solution)/shard_map/all_to_all | solution.py:54
  116.7 5.4 %all-to-all-start.1 = ((bf16[16,8,128,128]{3,2,1,0:T(8,128)(2,1)}), bf16[16,8,128,128]{3,2,1,0:T(8,128)(2,1)}, u32[]{:S(2)}, u32[]{:S(2)}) async-start(bf16[16,8,128,128]{3,2,1,0:T(8,128)(2,1)} %bitcast.69), calls=%async_computation.1 | async-start | bytes 8388608 | tf_op jit(solution)/shard_map/all_to_all | solution.py:56
  122.2 23.4 %fusion.2 = bf16[4096,1024]{1,0:T(8,128)(2,1)} fusion(bf16[2048,1024]{1,0:T(8,128)(2,1)} %all-gather.2.cloned.1.call-done, bf16[4096,1,2048]{2,0,1:T(8,128)(2,1)} %param.6), kind=kOutput, calls=%fused_computation.9 | convolution fusion | flops 17184063488 | bytes 29360128 | tf_op jit(solution)/shard_map/dot_general | solution.py:58
  145.6 35.8 %all-to-all-done.1 = bf16[16,8,128,128]{3,2,1,0:T(8,128)(2,1)} async-done(((bf16[16,8,128,128]{3,2,1,0:T(8,128)(2,1)}), bf16[16,8,128,128]{3,2,1,0:T(8,128)(2,1)}, u32[]{:S(2)}, u32[]{:S(2)}) %all-to-all-start.1) | async-done | bytes 4194336 | tf_op jit(solution)/shard_map/all_to_all | solution.py:56
  182.2 3.2 gather_fusion.5
  188.1 7.6 %all-to-all-start.4 = ((bf16[8,8,128,128]{3,1,2,0:T(8,128)(2,1)}), bf16[8,8,128,128]{3,1,2,0:T(8,128)(2,1)}, u32[]{:S(2)}, u32[]{:S(2)}) async-start(bf16[8,8,128,128]{3,1,2,0:T(8,128)(2,1)} %copy_select_fusion), calls=%async_computation.5 | async-start | bytes 4194304 | tf_op jit(solution)/shard_map/all_to_all | solution.py:75
  195.7 70.6 %reduce-scatter.2.cloned.1.call-done = bf16[256,1024]{1,0:T(8,128)(2,1)} async-done(((bf16[4096,1024]{1,0:T(8,128)(2,1)}), bf16[256,1024]{1,0:T(8,128)(2,1)}) %reduce-scatter.2.cloned.1.call-update) | async-done | bytes 524304 | tf_op jit(solution)/shard_map/reduce_scatter | solution.py:60
  266.3 3.8 convolution_bitcast_fusion
  270.2 5.2 %gather_fusion.4 = bf16[8,128,1536]{2,1,0:T(8,128)(2,1)} fusion(bf16[16,128,1536]{2,1,0:T(8,128)(2,1)} %all-to-all-done, s32[1024]{0:T(1024)S(1)} %pad_clamp_fusion), kind=kCustom, calls=%fused_computation.4 | custom fusion | bytes 6291488 | tf_op jit(solution)/shard_map/jit(_take)/gather | solution.py:67
  275.5 3.9 broadcast_select_fusion
  279.4 6.2 %all-to-all-start.3 = ((bf16[8,128,1536]{2,1,0:T(8,128)(2,1)}), bf16[8,128,1536]{2,1,0:T(8,128)(2,1)}, u32[]{:S(2)}, u32[]{:S(2)}) async-start(bf16[8,128,1536]{2,1,0:T(8,128)(2,1)} %broadcast_select_fusion), calls=%async_computation.4 | async-start | bytes 6291456 | tf_op jit(solution)/shard_map/all_to_all | solution.py:74
  288.4 85.6 %all-reduce.3.cloned.1.call-done = f32[1024,1024]{0,1:T(8,128)} async-done(((f32[1024,1024]{0,1:T(8,128)}), f32[1024,1024]{0,1:T(8,128)}) %all-reduce.3.cloned.1.call-update) | async-done | bytes 4194320 | tf_op jit(solution)/shard_map/psum | solution.py:13
  374.0 5.3 %all-to-all-start.2 = ((bf16[16,128,1024]{2,1,0:T(8,128)(2,1)}), bf16[16,128,1024]{2,1,0:T(8,128)(2,1)}, u32[]{:S(2)}, u32[]{:S(2)}) async-start(bf16[16,128,1024]{2,1,0:T(8,128)(2,1)} %gather_fusion.3), calls=%async_computation.3 | async-start | bytes 8388608 | tf_op jit(solution)/shard_map/all_to_all | solution.py:79
  379.3 58.8 %all-reduce.4 = bf16[1024,1024]{0,1:T(8,128)(2,1)} all-reduce(f32[1024,1024]{0,1:T(8,128)} %all-reduce.3.cloned.1.call-done), channel_id=1, replica_groups=mesh['row'=8,'col'=16] {'row'}, use_global_device_ids=true, to_apply=%region_4.5 | all-reduce | flops 1048576 | bytes 6291456 | tf_op jit(solution)/shard_map/psum | solution.py:13
  438.1 3.5 all-to-all-done.2
  446.1 6.1 %all-to-all-start.5 = ((bf16[8,128,1024]{2,1,0:T(8,128)(2,1)}), bf16[8,128,1024]{2,1,0:T(8,128)(2,1)}, u32[]{:S(2)}, u32[]{:S(2)}) async-start(bf16[8,128,1024]{2,1,0:T(8,128)(2,1)} %broadcast_select_fusion.1), calls=%async_computation.6 | async-start | bytes 4194304 | tf_op jit(solution)/shard_map/all_to_all | solution.py:83
  458.0 4.4 convolution_bitcast_fusion.1
  462.4 16.2 %all-to-all-done.5 = bf16[8,128,1024]{2,1,0:T(8,128)(2,1)} async-done(((bf16[8,128,1024]{2,1,0:T(8,128)(2,1)}), bf16[8,128,1024]{2,1,0:T(8,128)(2,1)}, u32[]{:S(2)}, u32[]{:S(2)}) %all-to-all-start.5) | async-done | bytes 2097184 | tf_op jit(solution)/shard_map/all_to_all | solution.py:83
  478.6 6.3 %convolution_convert_fusion = bf16[1024,512]{1,0:T(8,128)(2,1)S(1)} fusion(bf16[1,1,1024,512]{3,2,1,0:T(8,128)(2,1)S(1)} %copy-done, bf16[1024,1024]{1,0:T(8,128)(2,1)} %bitcast.22, bf16[1024,1024]{0,1:T(8,128)(2,1)} %all-reduce.4, bf16[1024,1536]{1,0:T(8,128)(2,1)} %bitcast.7), kind=kOutput, calls=%fused_computation.23 | convolution fusion | flops 3225944064 | bytes 8388608 | tf_op jit(solution)/shard_map/xm,xi->mi/dot_general | solution.py:94
  (52 shorter events, 28.3 us)
Async XLA Ops:
  7.2 445.0 %copy-start = (bf16[1,1,1024,512]{3,2,1,0:T(8,128)(2,1)S(1)}, bf16[1,1,1024,512]{3,2,1,0:T(8,128)(2,1)}, u32[]{:S(2)}) copy-start(bf16[1,1,1024,512]{3,2,1,0:T(8,128)(2,1)} %param.9) | copy-start | bytes 3145732
  7.2 115.0 %all-gather.2.cloned.1.call-start = ((), (), s32[]{:S(2)}) async-start(), calls=%async_computation.7 | async-start | bytes 4718592 | tf_op jit(solution)/shard_map/all_gather | solution.py:57
  15.9 100.8 %all-to-all-start = ((bf16[16,128,1536]{2,1,0:T(8,128)(2,1)}), bf16[16,128,1536]{2,1,0:T(8,128)(2,1)}, u32[]{:S(2)}, u32[]{:S(2)}) async-start(bf16[16,128,1536]{2,1,0:T(8,128)(2,1)} %gather_fusion.2), calls=%async_computation | async-start | bytes 12582912 | tf_op jit(solution)/shard_map/all_to_all | solution.py:54
  116.7 64.7 %all-to-all-start.1 = ((bf16[16,8,128,128]{3,2,1,0:T(8,128)(2,1)}), bf16[16,8,128,128]{3,2,1,0:T(8,128)(2,1)}, u32[]{:S(2)}, u32[]{:S(2)}) async-start(bf16[16,8,128,128]{3,2,1,0:T(8,128)(2,1)} %bitcast.69), calls=%async_computation.1 | async-start | bytes 8388608 | tf_op jit(solution)/shard_map/all_to_all | solution.py:56
  122.1 144.1 %reduce-scatter.2.cloned.1.call-start = ((), (), s32[]{:S(2)}) async-start(), calls=%async_computation.8 | async-start | bytes 8912896 | tf_op jit(solution)/shard_map/reduce_scatter | solution.py:60
  188.1 78.2 %copy-start.2 = (bf16[256,1024]{1,0:T(8,128)(2,1)S(1)}, bf16[256,1024]{1,0:T(8,128)(2,1)}, u32[]{:S(2)}) copy-start(bf16[256,1024]{1,0:T(8,128)(2,1)} %param.7) | copy-start | bytes 1572868
  188.1 91.3 %all-to-all-start.4 = ((bf16[8,8,128,128]{3,1,2,0:T(8,128)(2,1)}), bf16[8,8,128,128]{3,1,2,0:T(8,128)(2,1)}, u32[]{:S(2)}, u32[]{:S(2)}) async-start(bf16[8,8,128,128]{3,1,2,0:T(8,128)(2,1)} %copy_select_fusion), calls=%async_computation.5 | async-start | bytes 4194304 | tf_op jit(solution)/shard_map/all_to_all | solution.py:75
  195.7 178.3 %all-reduce.3.cloned.1.call-start = ((), (), s32[]{:S(2)}) async-start(), calls=%async_computation.9 | async-start | bytes 8388608 | tf_op jit(solution)/shard_map/psum | solution.py:13
  279.3 6.3 %copy-start.1 = (bf16[256,1024]{1,0:T(8,128)(2,1)S(1)}, bf16[256,1024]{1,0:T(8,128)(2,1)}, u32[]{:S(2)}) copy-start(bf16[256,1024]{1,0:T(8,128)(2,1)} %reduce-scatter.2.cloned.1.call-done) | copy-start | bytes 1572868
  279.4 94.6 %all-to-all-start.3 = ((bf16[8,128,1536]{2,1,0:T(8,128)(2,1)}), bf16[8,128,1536]{2,1,0:T(8,128)(2,1)}, u32[]{:S(2)}, u32[]{:S(2)}) async-start(bf16[8,128,1536]{2,1,0:T(8,128)(2,1)} %broadcast_select_fusion), calls=%async_computation.4 | async-start | bytes 6291456 | tf_op jit(solution)/shard_map/all_to_all | solution.py:74
  374.0 67.7 %all-to-all-start.2 = ((bf16[16,128,1024]{2,1,0:T(8,128)(2,1)}), bf16[16,128,1024]{2,1,0:T(8,128)(2,1)}, u32[]{:S(2)}, u32[]{:S(2)}) async-start(bf16[16,128,1024]{2,1,0:T(8,128)(2,1)} %gather_fusion.3), calls=%async_computation.3 | async-start | bytes 8388608 | tf_op jit(solution)/shard_map/all_to_all | solution.py:79
  446.1 32.5 %all-to-all-start.5 = ((bf16[8,128,1024]{2,1,0:T(8,128)(2,1)}), bf16[8,128,1024]{2,1,0:T(8,128)(2,1)}, u32[]{:S(2)}, u32[]{:S(2)}) async-start(bf16[8,128,1024]{2,1,0:T(8,128)(2,1)} %broadcast_select_fusion.1), calls=%async_computation.6 | async-start | bytes 4194304 | tf_op jit(solution)/shard_map/all_to_all | solution.py:83
  484.9 1.0 copy-start.3
Sparse Core Ops, SparseCore 0:
  9.7 35.7 all-gather.1
  181.5 84.6 reduce-scatter.1
  270.2 103.7 all-reduce.2
